TPU v7x, 512 devices: a whole 4x8x8 slice. The times are simulated.
512 devices in a mesh: seq: 64 (over z_hi, y, core), tp: 8 (over x, z_lo).
Axes of the slice: x: 4, y: 8, z: 8 (z_hi: 4, z_lo: 2; z = z_hi * 2 + z_lo), core: 2. Of those that a mesh axis runs over, the one named last changes fastest.
Arguments:
- query_proj: bfloat16 [16384, 3072], P('seq', 'tp'), may hold values from -8 to 8
- key_proj: bfloat16 [16384, 3072], P('seq', 'tp'), may hold values from -8 to 8
- value_proj: bfloat16 [16384, 3072], P('seq', 'tp'), may hold values from -6 to 6
- hidden: bfloat16 [16384, 3072], P('seq', 'tp'), may hold values from -2 to 2
- out_weight: bfloat16 [3072, 3072], P('tp'), may hold values from -0.109375 to 0.109375
- norm_gain: bfloat16 [3072], P('tp'), may hold values from 0.099609375 to 1.8984375
- segment_ids: int32 [16384], P('seq'), may hold values from 0 to 31, never falling along the last dimension, each value on 1 to 8192 neighbouring positions
- pad_mask: int32 [16384], P('seq'), may hold values 0 or 1
- page_table: int32 [128], P('seq'), may hold values from 0 to 1, as said below
Outputs:
- hidden_out: bfloat16 [16384, 3072], P('seq', 'tp')
- normed: bfloat16 [16384, 3072], P('seq', 'tp')
- kv_pages: bfloat16 [128, 2, 128, 3072], P('seq', None, None, 'tp')
Inputs may be any that keep to these rules, and one draw needn't show every extreme that they name: `segment_ids`: never falling along the tokens; each of the 32 prompts has 1 to 8192 tokens, one exactly 8192. `page_table`: the 2 pages of each aligned block of 2 pages name each slot once.
All inputs are finite; a program needn't handle non-finite values. No bound on the sum of `pad_mask` on one device may be relied on, other than what follows from the above.
Results may differ from a plain program's by a relative error of at most 0.014.
Values may be sent and summed in bfloat16 or wider, within the bound.
No kernel may reach another device: no remote copies, remote signals or barrier semaphores. Data moves between devices by JAX's collectives and lax.ppermute only.
A program may use at most 128 MiB of HBM per device.

v0:
```python
import math
import jax
import jax.numpy as jnp
from jax import lax
from jax.sharding import PartitionSpec as P

D = 3072
HEAD_DIM = 96
PAGE = 128
far_index = 1073741824
masked_score = -1e30
norm_epsilon = 1e-05


def passed_along(block, axis, distance):
    devices = range(lax.axis_size(axis))
    route = [(i - distance, i) for i in devices if i - distance in devices]
    return lax.ppermute(block, axis, route)


def rotate(values_in, position, head_count, head_dim):
    count_rows = values_in.shape[0]
    half_dim = head_dim // 2
    frequency = jnp.exp(
        jnp.arange(half_dim, dtype=jnp.float32) * (-2.0 * math.log(10000.0) / head_dim)
    )
    angles = position.astype(jnp.float32)[:, None] * frequency[None, :]
    cosine = jnp.cos(angles)[:, None, :]
    sine_part = jnp.sin(angles)[:, None, :]
    as_float = values_in.astype(jnp.float32).reshape(count_rows, head_count, head_dim)
    lower_half = as_float[..., :half_dim]
    upper_half = as_float[..., half_dim:]
    rotated = jnp.concatenate(
        [
            lower_half * cosine - upper_half * sine_part,
            upper_half * cosine + lower_half * sine_part,
        ],
        axis=-1,
    )
    return rotated.reshape(count_rows, head_count * head_dim).astype(jnp.bfloat16)


def attend(softmax_state, query_heads, block, visible):
    row_peak, row_total, weighted = softmax_state
    key_count = block.shape[1]
    head_count = query_heads.shape[1]
    key_heads = block[0].reshape(key_count, head_count, HEAD_DIM)
    val_heads = block[1].reshape(key_count, head_count, HEAD_DIM)
    factor = 1.0 / math.sqrt(HEAD_DIM)
    logits = (
        jnp.einsum("qhd,khd->hqk", query_heads, key_heads, preferred_element_type=jnp.float32)
        * factor
    )
    logits = jnp.where(visible[None], logits, masked_score)
    new_peak = jnp.maximum(row_peak, jnp.max(logits, axis=-1))
    rescale = jnp.exp(row_peak - new_peak)
    unnormed = jnp.where(visible[None], jnp.exp(logits - new_peak[..., None]), 0.0)
    row_total = row_total * rescale + jnp.sum(unnormed, axis=-1)
    weighted = weighted * rescale[..., None] + jnp.einsum(
        "hqk,khd->hqd", unnormed.astype(jnp.bfloat16), val_heads, preferred_element_type=jnp.float32
    )
    return (new_peak, row_total, weighted)


def per_device(
    query_proj,
    key_proj,
    value_proj,
    hidden,
    out_weight,
    norm_gain,
    segment_ids,
    pad_mask,
    page_table,
):
    tok_count = query_proj.shape[0]
    feat_count = query_proj.shape[1]
    head_count = feat_count // HEAD_DIM
    seg_count = lax.axis_size("seq") // 2
    reach_count = lax.axis_size("seq") // 2
    device_row = lax.axis_index("seq")
    tok_index = device_row * tok_count + jnp.arange(tok_count, dtype=jnp.int32)
    member = segment_ids[:, None] == jnp.arange(seg_count, dtype=jnp.int32)[None, :]
    local_first = jnp.min(jnp.where(member, tok_index[:, None], far_index), axis=0)
    first_tok = lax.pmin(local_first, "seq")
    position = tok_index - jnp.sum(jnp.where(member, first_tok[None, :], 0), axis=1)
    q_rot = rotate(query_proj, position, head_count, HEAD_DIM)
    k_rot = rotate(key_proj, position, head_count, HEAD_DIM)
    query_heads = q_rot.reshape(tok_count, head_count, HEAD_DIM)
    query_tag = segment_ids + 1
    key_tag = jnp.where(pad_mask == 1, segment_ids + 1, 0)
    own_block = jnp.stack([k_rot, value_proj])
    offsets = jnp.arange(tok_count, dtype=jnp.int32)
    own_visible = (key_tag[None, :] == query_tag[:, None]) & (
        offsets[None, :] <= offsets[:, None]
    ) | (offsets[None, :] == offsets[:, None])
    softmax_state = (
        jnp.full((head_count, tok_count), masked_score, jnp.float32),
        jnp.zeros((head_count, tok_count), jnp.float32),
        jnp.zeros((head_count, tok_count, HEAD_DIM), jnp.float32),
    )
    softmax_state = attend(softmax_state, query_heads, own_block, own_visible)

    def visit_block(current, moved, moved_tags):
        visible = moved_tags[None, :] == query_tag[:, None]
        return attend(current, query_heads, moved, visible)

    def cycle_turn(turn_index, loop_state):
        current, moved, moved_tags = loop_state
        moved, moved_tags = passed_along((moved, moved_tags), "seq", 1)
        return (visit_block(current, moved, moved_tags), moved, moved_tags)

    softmax_state = lax.fori_loop(0, reach_count, cycle_turn, (softmax_state, own_block, key_tag))[
        0
    ]
    row_peak, row_total, weighted = softmax_state
    attn = (
        jnp.transpose(weighted / row_total[..., None], (1, 0, 2))
        .reshape(tok_count, feat_count)
        .astype(jnp.bfloat16)
    )
    partial_value = jnp.dot(attn, out_weight, preferred_element_type=jnp.float32)
    feature_width = hidden.shape[1]
    summed = lax.psum(partial_value.astype(jnp.bfloat16), "tp").astype(jnp.float32)
    own_sum = lax.dynamic_slice_in_dim(
        summed, lax.axis_index("tp") * feature_width, feature_width, 1
    )
    hidden_out = (hidden.astype(jnp.float32) + own_sum).astype(jnp.bfloat16)
    stream_wide = hidden_out.astype(jnp.float32)
    square_total = lax.psum(jnp.sum(stream_wide * stream_wide, axis=1), "tp")
    normed = (
        stream_wide
        * lax.rsqrt(square_total / D + norm_epsilon)[:, None]
        * norm_gain.astype(jnp.float32)[None, :]
    ).astype(jnp.bfloat16)
    pad_scale = pad_mask.astype(jnp.bfloat16)[:, None]
    page_count = tok_count // PAGE
    stacked = jnp.stack([k_rot * pad_scale, value_proj * pad_scale])
    stacked = stacked.reshape(2, page_count, PAGE, feat_count).transpose(1, 0, 2, 3)
    kv_pages = jnp.zeros_like(stacked).at[page_table].set(stacked)
    return (hidden_out, normed, kv_pages)


def solution(mesh):
    placed = (
        P("seq", "tp"),
        P("seq", "tp"),
        P("seq", "tp"),
        P("seq", "tp"),
        P("tp", None),
        P("tp"),
        P("seq"),
        P("seq"),
        P("seq"),
    )
    return jax.shard_map(
        per_device,
        mesh=mesh,
        in_specs=placed,
        out_specs=(P("seq", "tp"), P("seq", "tp"), P("seq", None, None, "tp")),
        check_vma=False,
    )
```

profile of v0, /device:TPU:8, one launch (start us, length us, event | category | flops | bytes accessed | tf_op | source)
XLA Modules:
  0.0 713.5 jit_solution(16163749201808365648)
XLA Ops:
  8.2 28.3 %pmin.7 = s32[32]{0:T(128)S(1)} all-reduce(s32[32]{0:T(128)S(1)} %select_reduce_fusion.1), channel_id=1, replica_groups=mesh['seq'=64,'tp'=8] {'seq'}, use_global_device_ids=true, to_apply=%region_1.2 | all-reduce | flops 32 | bytes 256 | tf_op jit(solution)/shard_map/pmin | solution.py:85
  45.0 466.7 %while.18 = (s32[]{:T(128)}, f32[4,256]{1,0:T(4,128)S(1)}, f32[4,256]{1,0:T(4,128)S(1)}, f32[4,256,96]{1,2,0:T(8,128)S(1)}, bf16[2,256,384]{1,2,0:T(8,128)(2,1)}...) while((s32[]{:T(128)}, f32[4,256]{1,0:T(4,128)S(1)}, ...), condition=%wide.region_8.9_spmd, body=%wide.region_5.8_spmd.sunk | while | flops 103286784 | bytes 8003757 | solution.py:113
  153.3 4.9 collective-permute-start.1
  166.1 11.1 %collective-permute-start.1 = (s32[256]{0:T(256)}, s32[256]{0:T(256)S(1)}, u32[]{:S(2)}, u32[]{:S(2)}) collective-permute-start(s32[256]{0:T(256)} %get-tuple-element.160), channel_id=1, source_target_pairs={{0,8},{8,16},{16,24},{24,32},{32,40},{40,48},{48,56},{56,64},{64,7... | collective-permute-start | bytes 3080 | tf_op jit(solution)/shard_map/while/body/eval_jaxpr/ppermute | solution.py:18
  180.7 4.0 collective-permute-start
  184.7 11.4 %collective-permute-start.1 = (s32[256]{0:T(256)}, s32[256]{0:T(256)S(1)}, u32[]{:S(2)}, u32[]{:S(2)}) collective-permute-start(s32[256]{0:T(256)} %get-tuple-element.160), channel_id=1, source_target_pairs={{0,8},{8,16},{16,24},{24,32},{32,40},{40,48},{48,56},{56,64},{64,7... | collective-permute-start | bytes 3080 | tf_op jit(solution)/shard_map/while/body/eval_jaxpr/ppermute | solution.py:18
  199.5 4.0 collective-permute-start
  203.5 10.6 %collective-permute-start.1 = (s32[256]{0:T(256)}, s32[256]{0:T(256)S(1)}, u32[]{:S(2)}, u32[]{:S(2)}) collective-permute-start(s32[256]{0:T(256)} %get-tuple-element.160), channel_id=1, source_target_pairs={{0,8},{8,16},{16,24},{24,32},{32,40},{40,48},{48,56},{56,64},{64,7... | collective-permute-start | bytes 3080 | tf_op jit(solution)/shard_map/while/body/eval_jaxpr/ppermute | solution.py:18
  217.6 4.0 collective-permute-start
  221.6 9.2 %collective-permute-start.1 = (s32[256]{0:T(256)}, s32[256]{0:T(256)S(1)}, u32[]{:S(2)}, u32[]{:S(2)}) collective-permute-start(s32[256]{0:T(256)} %get-tuple-element.160), channel_id=1, source_target_pairs={{0,8},{8,16},{16,24},{24,32},{32,40},{40,48},{48,56},{56,64},{64,7... | collective-permute-start | bytes 3080 | tf_op jit(solution)/shard_map/while/body/eval_jaxpr/ppermute | solution.py:18
  234.3 4.0 collective-permute-start
  238.3 7.3 %collective-permute-start.1 = (s32[256]{0:T(256)}, s32[256]{0:T(256)S(1)}, u32[]{:S(2)}, u32[]{:S(2)}) collective-permute-start(s32[256]{0:T(256)} %get-tuple-element.160), channel_id=1, source_target_pairs={{0,8},{8,16},{16,24},{24,32},{32,40},{40,48},{48,56},{56,64},{64,7... | collective-permute-start | bytes 3080 | tf_op jit(solution)/shard_map/while/body/eval_jaxpr/ppermute | solution.py:18
  249.2 4.0 collective-permute-start
  253.2 7.3 %collective-permute-start.1 = (s32[256]{0:T(256)}, s32[256]{0:T(256)S(1)}, u32[]{:S(2)}, u32[]{:S(2)}) collective-permute-start(s32[256]{0:T(256)} %get-tuple-element.160), channel_id=1, source_target_pairs={{0,8},{8,16},{16,24},{24,32},{32,40},{40,48},{48,56},{56,64},{64,7... | collective-permute-start | bytes 3080 | tf_op jit(solution)/shard_map/while/body/eval_jaxpr/ppermute | solution.py:18
  264.0 4.0 collective-permute-start
  268.0 7.3 %collective-permute-start.1 = (s32[256]{0:T(256)}, s32[256]{0:T(256)S(1)}, u32[]{:S(2)}, u32[]{:S(2)}) collective-permute-start(s32[256]{0:T(256)} %get-tuple-element.160), channel_id=1, source_target_pairs={{0,8},{8,16},{16,24},{24,32},{32,40},{40,48},{48,56},{56,64},{64,7... | collective-permute-start | bytes 3080 | tf_op jit(solution)/shard_map/while/body/eval_jaxpr/ppermute | solution.py:18
  278.8 4.0 collective-permute-start
  282.8 7.3 %collective-permute-start.1 = (s32[256]{0:T(256)}, s32[256]{0:T(256)S(1)}, u32[]{:S(2)}, u32[]{:S(2)}) collective-permute-start(s32[256]{0:T(256)} %get-tuple-element.160), channel_id=1, source_target_pairs={{0,8},{8,16},{16,24},{24,32},{32,40},{40,48},{48,56},{56,64},{64,7... | collective-permute-start | bytes 3080 | tf_op jit(solution)/shard_map/while/body/eval_jaxpr/ppermute | solution.py:18
  293.7 4.0 collective-permute-start
  297.7 8.0 %collective-permute-start.1 = (s32[256]{0:T(256)}, s32[256]{0:T(256)S(1)}, u32[]{:S(2)}, u32[]{:S(2)}) collective-permute-start(s32[256]{0:T(256)} %get-tuple-element.160), channel_id=1, source_target_pairs={{0,8},{8,16},{16,24},{24,32},{32,40},{40,48},{48,56},{56,64},{64,7... | collective-permute-start | bytes 3080 | tf_op jit(solution)/shard_map/while/body/eval_jaxpr/ppermute | solution.py:18
  309.2 4.0 collective-permute-start
  313.3 8.0 %collective-permute-start.1 = (s32[256]{0:T(256)}, s32[256]{0:T(256)S(1)}, u32[]{:S(2)}, u32[]{:S(2)}) collective-permute-start(s32[256]{0:T(256)} %get-tuple-element.160), channel_id=1, source_target_pairs={{0,8},{8,16},{16,24},{24,32},{32,40},{40,48},{48,56},{56,64},{64,7... | collective-permute-start | bytes 3080 | tf_op jit(solution)/shard_map/while/body/eval_jaxpr/ppermute | solution.py:18
  324.8 4.0 collective-permute-start
  328.9 8.0 %collective-permute-start.1 = (s32[256]{0:T(256)}, s32[256]{0:T(256)S(1)}, u32[]{:S(2)}, u32[]{:S(2)}) collective-permute-start(s32[256]{0:T(256)} %get-tuple-element.160), channel_id=1, source_target_pairs={{0,8},{8,16},{16,24},{24,32},{32,40},{40,48},{48,56},{56,64},{64,7... | collective-permute-start | bytes 3080 | tf_op jit(solution)/shard_map/while/body/eval_jaxpr/ppermute | solution.py:18
  340.4 4.0 collective-permute-start
  344.5 8.0 %collective-permute-start.1 = (s32[256]{0:T(256)}, s32[256]{0:T(256)S(1)}, u32[]{:S(2)}, u32[]{:S(2)}) collective-permute-start(s32[256]{0:T(256)} %get-tuple-element.160), channel_id=1, source_target_pairs={{0,8},{8,16},{16,24},{24,32},{32,40},{40,48},{48,56},{56,64},{64,7... | collective-permute-start | bytes 3080 | tf_op jit(solution)/shard_map/while/body/eval_jaxpr/ppermute | solution.py:18
  356.0 4.0 collective-permute-start
  360.0 8.0 %collective-permute-start.1 = (s32[256]{0:T(256)}, s32[256]{0:T(256)S(1)}, u32[]{:S(2)}, u32[]{:S(2)}) collective-permute-start(s32[256]{0:T(256)} %get-tuple-element.160), channel_id=1, source_target_pairs={{0,8},{8,16},{16,24},{24,32},{32,40},{40,48},{48,56},{56,64},{64,7... | collective-permute-start | bytes 3080 | tf_op jit(solution)/shard_map/while/body/eval_jaxpr/ppermute | solution.py:18
  371.6 4.0 collective-permute-start
  375.6 8.0 %collective-permute-start.1 = (s32[256]{0:T(256)}, s32[256]{0:T(256)S(1)}, u32[]{:S(2)}, u32[]{:S(2)}) collective-permute-start(s32[256]{0:T(256)} %get-tuple-element.160), channel_id=1, source_target_pairs={{0,8},{8,16},{16,24},{24,32},{32,40},{40,48},{48,56},{56,64},{64,7... | collective-permute-start | bytes 3080 | tf_op jit(solution)/shard_map/while/body/eval_jaxpr/ppermute | solution.py:18
  387.1 4.0 collective-permute-start
  391.2 8.0 %collective-permute-start.1 = (s32[256]{0:T(256)}, s32[256]{0:T(256)S(1)}, u32[]{:S(2)}, u32[]{:S(2)}) collective-permute-start(s32[256]{0:T(256)} %get-tuple-element.160), channel_id=1, source_target_pairs={{0,8},{8,16},{16,24},{24,32},{32,40},{40,48},{48,56},{56,64},{64,7... | collective-permute-start | bytes 3080 | tf_op jit(solution)/shard_map/while/body/eval_jaxpr/ppermute | solution.py:18
  402.7 4.0 collective-permute-start
  406.8 8.0 %collective-permute-start.1 = (s32[256]{0:T(256)}, s32[256]{0:T(256)S(1)}, u32[]{:S(2)}, u32[]{:S(2)}) collective-permute-start(s32[256]{0:T(256)} %get-tuple-element.160), channel_id=1, source_target_pairs={{0,8},{8,16},{16,24},{24,32},{32,40},{40,48},{48,56},{56,64},{64,7... | collective-permute-start | bytes 3080 | tf_op jit(solution)/shard_map/while/body/eval_jaxpr/ppermute | solution.py:18
  418.3 4.0 collective-permute-start
  422.3 8.0 %collective-permute-start.1 = (s32[256]{0:T(256)}, s32[256]{0:T(256)S(1)}, u32[]{:S(2)}, u32[]{:S(2)}) collective-permute-start(s32[256]{0:T(256)} %get-tuple-element.160), channel_id=1, source_target_pairs={{0,8},{8,16},{16,24},{24,32},{32,40},{40,48},{48,56},{56,64},{64,7... | collective-permute-start | bytes 3080 | tf_op jit(solution)/shard_map/while/body/eval_jaxpr/ppermute | solution.py:18
  433.9 4.0 collective-permute-start
  437.9 8.0 %collective-permute-start.1 = (s32[256]{0:T(256)}, s32[256]{0:T(256)S(1)}, u32[]{:S(2)}, u32[]{:S(2)}) collective-permute-start(s32[256]{0:T(256)} %get-tuple-element.160), channel_id=1, source_target_pairs={{0,8},{8,16},{16,24},{24,32},{32,40},{40,48},{48,56},{56,64},{64,7... | collective-permute-start | bytes 3080 | tf_op jit(solution)/shard_map/while/body/eval_jaxpr/ppermute | solution.py:18
  449.5 4.0 collective-permute-start
  453.5 8.0 %collective-permute-start.1 = (s32[256]{0:T(256)}, s32[256]{0:T(256)S(1)}, u32[]{:S(2)}, u32[]{:S(2)}) collective-permute-start(s32[256]{0:T(256)} %get-tuple-element.160), channel_id=1, source_target_pairs={{0,8},{8,16},{16,24},{24,32},{32,40},{40,48},{48,56},{56,64},{64,7... | collective-permute-start | bytes 3080 | tf_op jit(solution)/shard_map/while/body/eval_jaxpr/ppermute | solution.py:18
  465.0 4.0 collective-permute-start
  469.1 8.0 %collective-permute-start.1 = (s32[256]{0:T(256)}, s32[256]{0:T(256)S(1)}, u32[]{:S(2)}, u32[]{:S(2)}) collective-permute-start(s32[256]{0:T(256)} %get-tuple-element.160), channel_id=1, source_target_pairs={{0,8},{8,16},{16,24},{24,32},{32,40},{40,48},{48,56},{56,64},{64,7... | collective-permute-start | bytes 3080 | tf_op jit(solution)/shard_map/while/body/eval_jaxpr/ppermute | solution.py:18
  480.6 4.0 collective-permute-start
  484.7 8.0 %collective-permute-start.1 = (s32[256]{0:T(256)}, s32[256]{0:T(256)S(1)}, u32[]{:S(2)}, u32[]{:S(2)}) collective-permute-start(s32[256]{0:T(256)} %get-tuple-element.160), channel_id=1, source_target_pairs={{0,8},{8,16},{16,24},{24,32},{32,40},{40,48},{48,56},{56,64},{64,7... | collective-permute-start | bytes 3080 | tf_op jit(solution)/shard_map/while/body/eval_jaxpr/ppermute | solution.py:18
  496.2 4.0 collective-permute-start
  500.2 8.0 %collective-permute-start.1 = (s32[256]{0:T(256)}, s32[256]{0:T(256)S(1)}, u32[]{:S(2)}, u32[]{:S(2)}) collective-permute-start(s32[256]{0:T(256)} %get-tuple-element.160), channel_id=1, source_target_pairs={{0,8},{8,16},{16,24},{24,32},{32,40},{40,48},{48,56},{56,64},{64,7... | collective-permute-start | bytes 3080 | tf_op jit(solution)/shard_map/while/body/eval_jaxpr/ppermute | solution.py:18
  515.4 171.0 %all-reduce.2.cloned.1.call-done = bf16[256,3072]{1,0:T(8,128)(2,1)} async-done(((bf16[256,3072]{1,0:T(8,128)(2,1)}), bf16[256,3072]{1,0:T(8,128)(2,1)}) %all-reduce.2.cloned.1.call-update) | async-done | bytes 1572880 | tf_op jit(solution)/shard_map/psum | solution.py:124
  687.5 18.4 %psum.15 = f32[256]{0:T(256)S(1)} all-reduce(f32[256]{0:T(256)S(1)} %get-tuple-element.66), channel_id=1, replica_groups=mesh['seq'=64,'tp'=8] {'tp'}, use_global_device_ids=true, to_apply=%region_11.12 | all-reduce | flops 256 | bytes 2048 | tf_op jit(solution)/shard_map/psum | solution.py:130
  (467 shorter events, 205.8 us)
Async XLA Ops:
  7.2 679.2 %all-reduce.2.cloned.1.call-start = ((), (), s32[]{:S(2)}) async-start(), calls=%async_computation | async-start | bytes 3145728 | tf_op jit(solution)/shard_map/psum | solution.py:124
  45.0 10.0 %collective-permute-start = (bf16[2,256,384]{1,2,0:T(8,128)(2,1)}, bf16[2,256,384]{1,2,0:T(8,128)(2,1)S(1)}, u32[]{:S(2)}, u32[]{:S(2)}) collective-permute-start(bf16[2,256,384]{1,2,0:T(8,128)(2,1)} %get-tuple-element.159), channel_id=1, source_target_pairs={{0,8},{8,16},{16,24},{24,32},{32,40},{40,48},{48,56},{56,64},{64,7... | collective-permute-start | bytes 1179656 | tf_op jit(solution)/shard_map/while/body/eval_jaxpr/ppermute | solution.py:18
  56.8 10.0 %collective-permute-start = (bf16[2,256,384]{1,2,0:T(8,128)(2,1)}, bf16[2,256,384]{1,2,0:T(8,128)(2,1)S(1)}, u32[]{:S(2)}, u32[]{:S(2)}) collective-permute-start(bf16[2,256,384]{1,2,0:T(8,128)(2,1)} %get-tuple-element.159), channel_id=1, source_target_pairs={{0,8},{8,16},{16,24},{24,32},{32,40},{40,48},{48,56},{56,64},{64,7... | collective-permute-start | bytes 1179656 | tf_op jit(solution)/shard_map/while/body/eval_jaxpr/ppermute | solution.py:18
  68.7 10.0 %collective-permute-start = (bf16[2,256,384]{1,2,0:T(8,128)(2,1)}, bf16[2,256,384]{1,2,0:T(8,128)(2,1)S(1)}, u32[]{:S(2)}, u32[]{:S(2)}) collective-permute-start(bf16[2,256,384]{1,2,0:T(8,128)(2,1)} %get-tuple-element.159), channel_id=1, source_target_pairs={{0,8},{8,16},{16,24},{24,32},{32,40},{40,48},{48,56},{56,64},{64,7... | collective-permute-start | bytes 1179656 | tf_op jit(solution)/shard_map/while/body/eval_jaxpr/ppermute | solution.py:18
  80.5 10.0 %collective-permute-start = (bf16[2,256,384]{1,2,0:T(8,128)(2,1)}, bf16[2,256,384]{1,2,0:T(8,128)(2,1)S(1)}, u32[]{:S(2)}, u32[]{:S(2)}) collective-permute-start(bf16[2,256,384]{1,2,0:T(8,128)(2,1)} %get-tuple-element.159), channel_id=1, source_target_pairs={{0,8},{8,16},{16,24},{24,32},{32,40},{40,48},{48,56},{56,64},{64,7... | collective-permute-start | bytes 1179656 | tf_op jit(solution)/shard_map/while/body/eval_jaxpr/ppermute | solution.py:18
  92.3 10.0 %collective-permute-start = (bf16[2,256,384]{1,2,0:T(8,128)(2,1)}, bf16[2,256,384]{1,2,0:T(8,128)(2,1)S(1)}, u32[]{:S(2)}, u32[]{:S(2)}) collective-permute-start(bf16[2,256,384]{1,2,0:T(8,128)(2,1)} %get-tuple-element.159), channel_id=1, source_target_pairs={{0,8},{8,16},{16,24},{24,32},{32,40},{40,48},{48,56},{56,64},{64,7... | collective-permute-start | bytes 1179656 | tf_op jit(solution)/shard_map/while/body/eval_jaxpr/ppermute | solution.py:18
  104.1 10.0 %collective-permute-start = (bf16[2,256,384]{1,2,0:T(8,128)(2,1)}, bf16[2,256,384]{1,2,0:T(8,128)(2,1)S(1)}, u32[]{:S(2)}, u32[]{:S(2)}) collective-permute-start(bf16[2,256,384]{1,2,0:T(8,128)(2,1)} %get-tuple-element.159), channel_id=1, source_target_pairs={{0,8},{8,16},{16,24},{24,32},{32,40},{40,48},{48,56},{56,64},{64,7... | collective-permute-start | bytes 1179656 | tf_op jit(solution)/shard_map/while/body/eval_jaxpr/ppermute | solution.py:18
  116.0 10.0 %collective-permute-start = (bf16[2,256,384]{1,2,0:T(8,128)(2,1)}, bf16[2,256,384]{1,2,0:T(8,128)(2,1)S(1)}, u32[]{:S(2)}, u32[]{:S(2)}) collective-permute-start(bf16[2,256,384]{1,2,0:T(8,128)(2,1)} %get-tuple-element.159), channel_id=1, source_target_pairs={{0,8},{8,16},{16,24},{24,32},{32,40},{40,48},{48,56},{56,64},{64,7... | collective-permute-start | bytes 1179656 | tf_op jit(solution)/shard_map/while/body/eval_jaxpr/ppermute | solution.py:18
  127.8 10.0 %collective-permute-start = (bf16[2,256,384]{1,2,0:T(8,128)(2,1)}, bf16[2,256,384]{1,2,0:T(8,128)(2,1)S(1)}, u32[]{:S(2)}, u32[]{:S(2)}) collective-permute-start(bf16[2,256,384]{1,2,0:T(8,128)(2,1)} %get-tuple-element.159), channel_id=1, source_target_pairs={{0,8},{8,16},{16,24},{24,32},{32,40},{40,48},{48,56},{56,64},{64,7... | collective-permute-start | bytes 1179656 | tf_op jit(solution)/shard_map/while/body/eval_jaxpr/ppermute | solution.py:18
  139.6 10.0 %collective-permute-start = (bf16[2,256,384]{1,2,0:T(8,128)(2,1)}, bf16[2,256,384]{1,2,0:T(8,128)(2,1)S(1)}, u32[]{:S(2)}, u32[]{:S(2)}) collective-permute-start(bf16[2,256,384]{1,2,0:T(8,128)(2,1)} %get-tuple-element.159), channel_id=1, source_target_pairs={{0,8},{8,16},{16,24},{24,32},{32,40},{40,48},{48,56},{56,64},{64,7... | collective-permute-start | bytes 1179656 | tf_op jit(solution)/shard_map/while/body/eval_jaxpr/ppermute | solution.py:18
  151.4 10.0 %collective-permute-start = (bf16[2,256,384]{1,2,0:T(8,128)(2,1)}, bf16[2,256,384]{1,2,0:T(8,128)(2,1)S(1)}, u32[]{:S(2)}, u32[]{:S(2)}) collective-permute-start(bf16[2,256,384]{1,2,0:T(8,128)(2,1)} %get-tuple-element.159), channel_id=1, source_target_pairs={{0,8},{8,16},{16,24},{24,32},{32,40},{40,48},{48,56},{56,64},{64,7... | collective-permute-start | bytes 1179656 | tf_op jit(solution)/shard_map/while/body/eval_jaxpr/ppermute | solution.py:18
  163.3 15.6 %collective-permute-start = (bf16[2,256,384]{1,2,0:T(8,128)(2,1)}, bf16[2,256,384]{1,2,0:T(8,128)(2,1)S(1)}, u32[]{:S(2)}, u32[]{:S(2)}) collective-permute-start(bf16[2,256,384]{1,2,0:T(8,128)(2,1)} %get-tuple-element.159), channel_id=1, source_target_pairs={{0,8},{8,16},{16,24},{24,32},{32,40},{40,48},{48,56},{56,64},{64,7... | collective-permute-start | bytes 1179656 | tf_op jit(solution)/shard_map/while/body/eval_jaxpr/ppermute | solution.py:18
  166.1 12.1 %collective-permute-start.1 = (s32[256]{0:T(256)}, s32[256]{0:T(256)S(1)}, u32[]{:S(2)}, u32[]{:S(2)}) collective-permute-start(s32[256]{0:T(256)} %get-tuple-element.160), channel_id=1, source_target_pairs={{0,8},{8,16},{16,24},{24,32},{32,40},{40,48},{48,56},{56,64},{64,7... | collective-permute-start | bytes 3080 | tf_op jit(solution)/shard_map/while/body/eval_jaxpr/ppermute | solution.py:18
  180.7 17.1 %collective-permute-start = (bf16[2,256,384]{1,2,0:T(8,128)(2,1)}, bf16[2,256,384]{1,2,0:T(8,128)(2,1)S(1)}, u32[]{:S(2)}, u32[]{:S(2)}) collective-permute-start(bf16[2,256,384]{1,2,0:T(8,128)(2,1)} %get-tuple-element.159), channel_id=1, source_target_pairs={{0,8},{8,16},{16,24},{24,32},{32,40},{40,48},{48,56},{56,64},{64,7... | collective-permute-start | bytes 1179656 | tf_op jit(solution)/shard_map/while/body/eval_jaxpr/ppermute | solution.py:18
  184.7 12.4 %collective-permute-start.1 = (s32[256]{0:T(256)}, s32[256]{0:T(256)S(1)}, u32[]{:S(2)}, u32[]{:S(2)}) collective-permute-start(s32[256]{0:T(256)} %get-tuple-element.160), channel_id=1, source_target_pairs={{0,8},{8,16},{16,24},{24,32},{32,40},{40,48},{48,56},{56,64},{64,7... | collective-permute-start | bytes 3080 | tf_op jit(solution)/shard_map/while/body/eval_jaxpr/ppermute | solution.py:18
  199.5 16.3 %collective-permute-start = (bf16[2,256,384]{1,2,0:T(8,128)(2,1)}, bf16[2,256,384]{1,2,0:T(8,128)(2,1)S(1)}, u32[]{:S(2)}, u32[]{:S(2)}) collective-permute-start(bf16[2,256,384]{1,2,0:T(8,128)(2,1)} %get-tuple-element.159), channel_id=1, source_target_pairs={{0,8},{8,16},{16,24},{24,32},{32,40},{40,48},{48,56},{56,64},{64,7... | collective-permute-start | bytes 1179656 | tf_op jit(solution)/shard_map/while/body/eval_jaxpr/ppermute | solution.py:18
  203.5 11.6 %collective-permute-start.1 = (s32[256]{0:T(256)}, s32[256]{0:T(256)S(1)}, u32[]{:S(2)}, u32[]{:S(2)}) collective-permute-start(s32[256]{0:T(256)} %get-tuple-element.160), channel_id=1, source_target_pairs={{0,8},{8,16},{16,24},{24,32},{32,40},{40,48},{48,56},{56,64},{64,7... | collective-permute-start | bytes 3080 | tf_op jit(solution)/shard_map/while/body/eval_jaxpr/ppermute | solution.py:18
  217.6 14.9 %collective-permute-start = (bf16[2,256,384]{1,2,0:T(8,128)(2,1)}, bf16[2,256,384]{1,2,0:T(8,128)(2,1)S(1)}, u32[]{:S(2)}, u32[]{:S(2)}) collective-permute-start(bf16[2,256,384]{1,2,0:T(8,128)(2,1)} %get-tuple-element.159), channel_id=1, source_target_pairs={{0,8},{8,16},{16,24},{24,32},{32,40},{40,48},{48,56},{56,64},{64,7... | collective-permute-start | bytes 1179656 | tf_op jit(solution)/shard_map/while/body/eval_jaxpr/ppermute | solution.py:18
  221.6 10.2 %collective-permute-start.1 = (s32[256]{0:T(256)}, s32[256]{0:T(256)S(1)}, u32[]{:S(2)}, u32[]{:S(2)}) collective-permute-start(s32[256]{0:T(256)} %get-tuple-element.160), channel_id=1, source_target_pairs={{0,8},{8,16},{16,24},{24,32},{32,40},{40,48},{48,56},{56,64},{64,7... | collective-permute-start | bytes 3080 | tf_op jit(solution)/shard_map/while/body/eval_jaxpr/ppermute | solution.py:18
  234.3 13.0 %collective-permute-start = (bf16[2,256,384]{1,2,0:T(8,128)(2,1)}, bf16[2,256,384]{1,2,0:T(8,128)(2,1)S(1)}, u32[]{:S(2)}, u32[]{:S(2)}) collective-permute-start(bf16[2,256,384]{1,2,0:T(8,128)(2,1)} %get-tuple-element.159), channel_id=1, source_target_pairs={{0,8},{8,16},{16,24},{24,32},{32,40},{40,48},{48,56},{56,64},{64,7... | collective-permute-start | bytes 1179656 | tf_op jit(solution)/shard_map/while/body/eval_jaxpr/ppermute | solution.py:18
  249.2 13.0 %collective-permute-start = (bf16[2,256,384]{1,2,0:T(8,128)(2,1)}, bf16[2,256,384]{1,2,0:T(8,128)(2,1)S(1)}, u32[]{:S(2)}, u32[]{:S(2)}) collective-permute-start(bf16[2,256,384]{1,2,0:T(8,128)(2,1)} %get-tuple-element.159), channel_id=1, source_target_pairs={{0,8},{8,16},{16,24},{24,32},{32,40},{40,48},{48,56},{56,64},{64,7... | collective-permute-start | bytes 1179656 | tf_op jit(solution)/shard_map/while/body/eval_jaxpr/ppermute | solution.py:18
  264.0 13.0 %collective-permute-start = (bf16[2,256,384]{1,2,0:T(8,128)(2,1)}, bf16[2,256,384]{1,2,0:T(8,128)(2,1)S(1)}, u32[]{:S(2)}, u32[]{:S(2)}) collective-permute-start(bf16[2,256,384]{1,2,0:T(8,128)(2,1)} %get-tuple-element.159), channel_id=1, source_target_pairs={{0,8},{8,16},{16,24},{24,32},{32,40},{40,48},{48,56},{56,64},{64,7... | collective-permute-start | bytes 1179656 | tf_op jit(solution)/shard_map/while/body/eval_jaxpr/ppermute | solution.py:18
  278.8 13.0 %collective-permute-start = (bf16[2,256,384]{1,2,0:T(8,128)(2,1)}, bf16[2,256,384]{1,2,0:T(8,128)(2,1)S(1)}, u32[]{:S(2)}, u32[]{:S(2)}) collective-permute-start(bf16[2,256,384]{1,2,0:T(8,128)(2,1)} %get-tuple-element.159), channel_id=1, source_target_pairs={{0,8},{8,16},{16,24},{24,32},{32,40},{40,48},{48,56},{56,64},{64,7... | collective-permute-start | bytes 1179656 | tf_op jit(solution)/shard_map/while/body/eval_jaxpr/ppermute | solution.py:18
  293.7 13.8 %collective-permute-start = (bf16[2,256,384]{1,2,0:T(8,128)(2,1)}, bf16[2,256,384]{1,2,0:T(8,128)(2,1)S(1)}, u32[]{:S(2)}, u32[]{:S(2)}) collective-permute-start(bf16[2,256,384]{1,2,0:T(8,128)(2,1)} %get-tuple-element.159), channel_id=1, source_target_pairs={{0,8},{8,16},{16,24},{24,32},{32,40},{40,48},{48,56},{56,64},{64,7... | collective-permute-start | bytes 1179656 | tf_op jit(solution)/shard_map/while/body/eval_jaxpr/ppermute | solution.py:18
  297.7 9.1 %collective-permute-start.1 = (s32[256]{0:T(256)}, s32[256]{0:T(256)S(1)}, u32[]{:S(2)}, u32[]{:S(2)}) collective-permute-start(s32[256]{0:T(256)} %get-tuple-element.160), channel_id=1, source_target_pairs={{0,8},{8,16},{16,24},{24,32},{32,40},{40,48},{48,56},{56,64},{64,7... | collective-permute-start | bytes 3080 | tf_op jit(solution)/shard_map/while/body/eval_jaxpr/ppermute | solution.py:18
  309.2 13.8 %collective-permute-start = (bf16[2,256,384]{1,2,0:T(8,128)(2,1)}, bf16[2,256,384]{1,2,0:T(8,128)(2,1)S(1)}, u32[]{:S(2)}, u32[]{:S(2)}) collective-permute-start(bf16[2,256,384]{1,2,0:T(8,128)(2,1)} %get-tuple-element.159), channel_id=1, source_target_pairs={{0,8},{8,16},{16,24},{24,32},{32,40},{40,48},{48,56},{56,64},{64,7... | collective-permute-start | bytes 1179656 | tf_op jit(solution)/shard_map/while/body/eval_jaxpr/ppermute | solution.py:18
  313.3 9.1 %collective-permute-start.1 = (s32[256]{0:T(256)}, s32[256]{0:T(256)S(1)}, u32[]{:S(2)}, u32[]{:S(2)}) collective-permute-start(s32[256]{0:T(256)} %get-tuple-element.160), channel_id=1, source_target_pairs={{0,8},{8,16},{16,24},{24,32},{32,40},{40,48},{48,56},{56,64},{64,7... | collective-permute-start | bytes 3080 | tf_op jit(solution)/shard_map/while/body/eval_jaxpr/ppermute | solution.py:18
  324.8 13.8 %collective-permute-start = (bf16[2,256,384]{1,2,0:T(8,128)(2,1)}, bf16[2,256,384]{1,2,0:T(8,128)(2,1)S(1)}, u32[]{:S(2)}, u32[]{:S(2)}) collective-permute-start(bf16[2,256,384]{1,2,0:T(8,128)(2,1)} %get-tuple-element.159), channel_id=1, source_target_pairs={{0,8},{8,16},{16,24},{24,32},{32,40},{40,48},{48,56},{56,64},{64,7... | collective-permute-start | bytes 1179656 | tf_op jit(solution)/shard_map/while/body/eval_jaxpr/ppermute | solution.py:18
  328.9 9.1 %collective-permute-start.1 = (s32[256]{0:T(256)}, s32[256]{0:T(256)S(1)}, u32[]{:S(2)}, u32[]{:S(2)}) collective-permute-start(s32[256]{0:T(256)} %get-tuple-element.160), channel_id=1, source_target_pairs={{0,8},{8,16},{16,24},{24,32},{32,40},{40,48},{48,56},{56,64},{64,7... | collective-permute-start | bytes 3080 | tf_op jit(solution)/shard_map/while/body/eval_jaxpr/ppermute | solution.py:18
  340.4 13.8 %collective-permute-start = (bf16[2,256,384]{1,2,0:T(8,128)(2,1)}, bf16[2,256,384]{1,2,0:T(8,128)(2,1)S(1)}, u32[]{:S(2)}, u32[]{:S(2)}) collective-permute-start(bf16[2,256,384]{1,2,0:T(8,128)(2,1)} %get-tuple-element.159), channel_id=1, source_target_pairs={{0,8},{8,16},{16,24},{24,32},{32,40},{40,48},{48,56},{56,64},{64,7... | collective-permute-start | bytes 1179656 | tf_op jit(solution)/shard_map/while/body/eval_jaxpr/ppermute | solution.py:18
  344.5 9.1 %collective-permute-start.1 = (s32[256]{0:T(256)}, s32[256]{0:T(256)S(1)}, u32[]{:S(2)}, u32[]{:S(2)}) collective-permute-start(s32[256]{0:T(256)} %get-tuple-element.160), channel_id=1, source_target_pairs={{0,8},{8,16},{16,24},{24,32},{32,40},{40,48},{48,56},{56,64},{64,7... | collective-permute-start | bytes 3080 | tf_op jit(solution)/shard_map/while/body/eval_jaxpr/ppermute | solution.py:18
  356.0 13.8 %collective-permute-start = (bf16[2,256,384]{1,2,0:T(8,128)(2,1)}, bf16[2,256,384]{1,2,0:T(8,128)(2,1)S(1)}, u32[]{:S(2)}, u32[]{:S(2)}) collective-permute-start(bf16[2,256,384]{1,2,0:T(8,128)(2,1)} %get-tuple-element.159), channel_id=1, source_target_pairs={{0,8},{8,16},{16,24},{24,32},{32,40},{40,48},{48,56},{56,64},{64,7... | collective-permute-start | bytes 1179656 | tf_op jit(solution)/shard_map/while/body/eval_jaxpr/ppermute | solution.py:18
  360.0 9.1 %collective-permute-start.1 = (s32[256]{0:T(256)}, s32[256]{0:T(256)S(1)}, u32[]{:S(2)}, u32[]{:S(2)}) collective-permute-start(s32[256]{0:T(256)} %get-tuple-element.160), channel_id=1, source_target_pairs={{0,8},{8,16},{16,24},{24,32},{32,40},{40,48},{48,56},{56,64},{64,7... | collective-permute-start | bytes 3080 | tf_op jit(solution)/shard_map/while/body/eval_jaxpr/ppermute | solution.py:18
  371.6 13.8 %collective-permute-start = (bf16[2,256,384]{1,2,0:T(8,128)(2,1)}, bf16[2,256,384]{1,2,0:T(8,128)(2,1)S(1)}, u32[]{:S(2)}, u32[]{:S(2)}) collective-permute-start(bf16[2,256,384]{1,2,0:T(8,128)(2,1)} %get-tuple-element.159), channel_id=1, source_target_pairs={{0,8},{8,16},{16,24},{24,32},{32,40},{40,48},{48,56},{56,64},{64,7... | collective-permute-start | bytes 1179656 | tf_op jit(solution)/shard_map/while/body/eval_jaxpr/ppermute | solution.py:18
  375.6 9.1 %collective-permute-start.1 = (s32[256]{0:T(256)}, s32[256]{0:T(256)S(1)}, u32[]{:S(2)}, u32[]{:S(2)}) collective-permute-start(s32[256]{0:T(256)} %get-tuple-element.160), channel_id=1, source_target_pairs={{0,8},{8,16},{16,24},{24,32},{32,40},{40,48},{48,56},{56,64},{64,7... | collective-permute-start | bytes 3080 | tf_op jit(solution)/shard_map/while/body/eval_jaxpr/ppermute | solution.py:18
  387.1 13.8 %collective-permute-start = (bf16[2,256,384]{1,2,0:T(8,128)(2,1)}, bf16[2,256,384]{1,2,0:T(8,128)(2,1)S(1)}, u32[]{:S(2)}, u32[]{:S(2)}) collective-permute-start(bf16[2,256,384]{1,2,0:T(8,128)(2,1)} %get-tuple-element.159), channel_id=1, source_target_pairs={{0,8},{8,16},{16,24},{24,32},{32,40},{40,48},{48,56},{56,64},{64,7... | collective-permute-start | bytes 1179656 | tf_op jit(solution)/shard_map/while/body/eval_jaxpr/ppermute | solution.py:18
  391.2 9.1 %collective-permute-start.1 = (s32[256]{0:T(256)}, s32[256]{0:T(256)S(1)}, u32[]{:S(2)}, u32[]{:S(2)}) collective-permute-start(s32[256]{0:T(256)} %get-tuple-element.160), channel_id=1, source_target_pairs={{0,8},{8,16},{16,24},{24,32},{32,40},{40,48},{48,56},{56,64},{64,7... | collective-permute-start | bytes 3080 | tf_op jit(solution)/shard_map/while/body/eval_jaxpr/ppermute | solution.py:18
  402.7 13.8 %collective-permute-start = (bf16[2,256,384]{1,2,0:T(8,128)(2,1)}, bf16[2,256,384]{1,2,0:T(8,128)(2,1)S(1)}, u32[]{:S(2)}, u32[]{:S(2)}) collective-permute-start(bf16[2,256,384]{1,2,0:T(8,128)(2,1)} %get-tuple-element.159), channel_id=1, source_target_pairs={{0,8},{8,16},{16,24},{24,32},{32,40},{40,48},{48,56},{56,64},{64,7... | collective-permute-start | bytes 1179656 | tf_op jit(solution)/shard_map/while/body/eval_jaxpr/ppermute | solution.py:18
  406.8 9.1 %collective-permute-start.1 = (s32[256]{0:T(256)}, s32[256]{0:T(256)S(1)}, u32[]{:S(2)}, u32[]{:S(2)}) collective-permute-start(s32[256]{0:T(256)} %get-tuple-element.160), channel_id=1, source_target_pairs={{0,8},{8,16},{16,24},{24,32},{32,40},{40,48},{48,56},{56,64},{64,7... | collective-permute-start | bytes 3080 | tf_op jit(solution)/shard_map/while/body/eval_jaxpr/ppermute | solution.py:18
  418.3 13.8 %collective-permute-start = (bf16[2,256,384]{1,2,0:T(8,128)(2,1)}, bf16[2,256,384]{1,2,0:T(8,128)(2,1)S(1)}, u32[]{:S(2)}, u32[]{:S(2)}) collective-permute-start(bf16[2,256,384]{1,2,0:T(8,128)(2,1)} %get-tuple-element.159), channel_id=1, source_target_pairs={{0,8},{8,16},{16,24},{24,32},{32,40},{40,48},{48,56},{56,64},{64,7... | collective-permute-start | bytes 1179656 | tf_op jit(solution)/shard_map/while/body/eval_jaxpr/ppermute | solution.py:18
  422.3 9.1 %collective-permute-start.1 = (s32[256]{0:T(256)}, s32[256]{0:T(256)S(1)}, u32[]{:S(2)}, u32[]{:S(2)}) collective-permute-start(s32[256]{0:T(256)} %get-tuple-element.160), channel_id=1, source_target_pairs={{0,8},{8,16},{16,24},{24,32},{32,40},{40,48},{48,56},{56,64},{64,7... | collective-permute-start | bytes 3080 | tf_op jit(solution)/shard_map/while/body/eval_jaxpr/ppermute | solution.py:18
  433.9 13.8 %collective-permute-start = (bf16[2,256,384]{1,2,0:T(8,128)(2,1)}, bf16[2,256,384]{1,2,0:T(8,128)(2,1)S(1)}, u32[]{:S(2)}, u32[]{:S(2)}) collective-permute-start(bf16[2,256,384]{1,2,0:T(8,128)(2,1)} %get-tuple-element.159), channel_id=1, source_target_pairs={{0,8},{8,16},{16,24},{24,32},{32,40},{40,48},{48,56},{56,64},{64,7... | collective-permute-start | bytes 1179656 | tf_op jit(solution)/shard_map/while/body/eval_jaxpr/ppermute | solution.py:18
  449.5 13.8 %collective-permute-start = (bf16[2,256,384]{1,2,0:T(8,128)(2,1)}, bf16[2,256,384]{1,2,0:T(8,128)(2,1)S(1)}, u32[]{:S(2)}, u32[]{:S(2)}) collective-permute-start(bf16[2,256,384]{1,2,0:T(8,128)(2,1)} %get-tuple-element.159), channel_id=1, source_target_pairs={{0,8},{8,16},{16,24},{24,32},{32,40},{40,48},{48,56},{56,64},{64,7... | collective-permute-start | bytes 1179656 | tf_op jit(solution)/shard_map/while/body/eval_jaxpr/ppermute | solution.py:18
  453.5 9.1 %collective-permute-start.1 = (s32[256]{0:T(256)}, s32[256]{0:T(256)S(1)}, u32[]{:S(2)}, u32[]{:S(2)}) collective-permute-start(s32[256]{0:T(256)} %get-tuple-element.160), channel_id=1, source_target_pairs={{0,8},{8,16},{16,24},{24,32},{32,40},{40,48},{48,56},{56,64},{64,7... | collective-permute-start | bytes 3080 | tf_op jit(solution)/shard_map/while/body/eval_jaxpr/ppermute | solution.py:18
  465.0 13.8 %collective-permute-start = (bf16[2,256,384]{1,2,0:T(8,128)(2,1)}, bf16[2,256,384]{1,2,0:T(8,128)(2,1)S(1)}, u32[]{:S(2)}, u32[]{:S(2)}) collective-permute-start(bf16[2,256,384]{1,2,0:T(8,128)(2,1)} %get-tuple-element.159), channel_id=1, source_target_pairs={{0,8},{8,16},{16,24},{24,32},{32,40},{40,48},{48,56},{56,64},{64,7... | collective-permute-start | bytes 1179656 | tf_op jit(solution)/shard_map/while/body/eval_jaxpr/ppermute | solution.py:18
  480.6 13.8 %collective-permute-start = (bf16[2,256,384]{1,2,0:T(8,128)(2,1)}, bf16[2,256,384]{1,2,0:T(8,128)(2,1)S(1)}, u32[]{:S(2)}, u32[]{:S(2)}) collective-permute-start(bf16[2,256,384]{1,2,0:T(8,128)(2,1)} %get-tuple-element.159), channel_id=1, source_target_pairs={{0,8},{8,16},{16,24},{24,32},{32,40},{40,48},{48,56},{56,64},{64,7... | collective-permute-start | bytes 1179656 | tf_op jit(solution)/shard_map/while/body/eval_jaxpr/ppermute | solution.py:18
  496.2 13.8 %collective-permute-start = (bf16[2,256,384]{1,2,0:T(8,128)(2,1)}, bf16[2,256,384]{1,2,0:T(8,128)(2,1)S(1)}, u32[]{:S(2)}, u32[]{:S(2)}) collective-permute-start(bf16[2,256,384]{1,2,0:T(8,128)(2,1)} %get-tuple-element.159), channel_id=1, source_target_pairs={{0,8},{8,16},{16,24},{24,32},{32,40},{40,48},{48,56},{56,64},{64,7... | collective-permute-start | bytes 1179656 | tf_op jit(solution)/shard_map/while/body/eval_jaxpr/ppermute | solution.py:18
  500.2 9.1 %collective-permute-start.1 = (s32[256]{0:T(256)}, s32[256]{0:T(256)S(1)}, u32[]{:S(2)}, u32[]{:S(2)}) collective-permute-start(s32[256]{0:T(256)} %get-tuple-element.160), channel_id=1, source_target_pairs={{0,8},{8,16},{16,24},{24,32},{32,40},{40,48},{48,56},{56,64},{64,7... | collective-permute-start | bytes 3080 | tf_op jit(solution)/shard_map/while/body/eval_jaxpr/ppermute | solution.py:18
  (30 other events, 1099.8 us)
Sparse Core Ops, SparseCore 0:
  514.2 172.1 all-reduce.1
where the time goes:
time: 716 us; the launch traced here: 713 us
  starting transfers between devices  327 us (46%)
  waiting for transfers between devices  231 us (32%)
  local copies, waits for them, and re-layouts  47.7 us (7%)
  blocking collectives  46.6 us (7%)
  matrix products  28 us (4%)
  other arithmetic  16.5 us (2%)
  between operations  14.3 us (2%)
    ppermute x64, starting transfers between devices, passed_along(): return lax.ppermute(block, axis, route)  327 us
    psum x1, waiting for transfers between devices, per_device(): lax.psum(partial_value.astype(jnp.bfloat16), 'tp').astype(jnp.float32)  171 us
    ppermute x64, waiting for transfers between devices, passed_along(): return lax.ppermute(block, axis, route)  59.6 us
    while x96, local copies, waits for them, and re-layouts  42 us
    pmin x1, blocking collectives, per_device(): first_tok = lax.pmin(local_first, 'seq')  28.3 us
    psum x1, blocking collectives, per_device(): square_total = lax.psum(jnp.sum(stream_wide * stream_wide, axis=1), 'tp')  18.4 us
  transfers between devices with their start and end apart: 65, of which 33 were waited for; matrix products, arithmetic and copies ran while one was open for 3% of the time, Pallas kernels for 0%

commit v1 on v0

--- a/solution.py
+++ b/solution.py
@@ -1,3 +1,4 @@
+import functools
 import math
 import jax
 import jax.numpy as jnp
@@ -10,6 +11,13 @@
 far_index = 1073741824
 masked_score = -1e30
 norm_epsilon = 1e-05
+
+
+def obtain_knots(x_part, axis_key):
+    return jnp.sum(jax.lax.all_gather(x_part, axis_name=axis_key), 0)
+
+
+play_body = functools.partial(obtain_knots, axis_key="tp")
 
 
 def passed_along(block, axis, distance):
@@ -121,7 +129,7 @@
     )
     partial_value = jnp.dot(attn, out_weight, preferred_element_type=jnp.float32)
     feature_width = hidden.shape[1]
-    summed = lax.psum(partial_value.astype(jnp.bfloat16), "tp").astype(jnp.float32)
+    summed = play_body(partial_value.astype(jnp.bfloat16)).astype(jnp.float32)
     own_sum = lax.dynamic_slice_in_dim(
         summed, lax.axis_index("tp") * feature_width, feature_width, 1
     )

time: 716 us -> 879 us (1.23)
  waiting for transfers between devices: 231 us -> 385 us
  other arithmetic: 16.5 us -> 25.4 us
    all_gather x0 -> x1, waiting for transfers between devices: none -> 326 us  [obtain_knots(): return jnp.sum(jax.lax.all_gather(x_part, axis_name=axis_key), 0)]
    psum x1 -> x0, waiting for transfers between devices: 171 us -> none  [per_device(): lax.psum(partial_value.astype(jnp.bfloat16), 'tp').astype(jnp.float32)]
where the time goes in v1:
time: 879 us; the launch traced here: 876 us
  waiting for transfers between devices  385 us (44%)
  starting transfers between devices  327 us (37%)
  local copies, waits for them, and re-layouts  47.7 us (5%)
  blocking collectives  46.8 us (5%)
  matrix products  28.1 us (3%)
  other arithmetic  25.4 us (3%)
  between operations  14.3 us (2%)
    ppermute x64, starting transfers between devices, passed_along(): return lax.ppermute(block, axis, route)  326 us
    all_gather x1, waiting for transfers between devices, obtain_knots(): return jnp.sum(jax.lax.all_gather(x_part, axis_name=axis_key), 0)  326 us
    ppermute x64, waiting for transfers between devices, passed_along(): return lax.ppermute(block, axis, route)  59.6 us
    while x96, local copies, waits for them, and re-layouts  42 us
    pmin x1, blocking collectives, per_device(): first_tok = lax.pmin(local_first, 'seq')  28.3 us
    psum x1, blocking collectives, per_device(): square_total = lax.psum(jnp.sum(stream_wide * stream_wide, axis=1), 'tp')  18.5 us
  transfers between devices with their start and end apart: 65, of which 33 were waited for; matrix products, arithmetic and copies ran while one was open for 3% of the time, Pallas kernels for 0%

profile of v1, /device:TPU:8, one launch (start us, length us, event | category | flops | bytes accessed | tf_op | source)
XLA Modules:
  0.0 876.4 jit_solution(2473615842424118880)
XLA Ops:
  8.2 28.3 %pmin.7 = s32[32]{0:T(128)S(1)} all-reduce(s32[32]{0:T(128)S(1)} %select_reduce_fusion.1), channel_id=1, replica_groups=mesh['seq'=64,'tp'=8] {'seq'}, use_global_device_ids=true, to_apply=%region_1.2 | all-reduce | flops 32 | bytes 256 | tf_op jit(solution)/shard_map/pmin | solution.py:93
  45.1 465.9 %while.18 = (s32[]{:T(128)}, f32[4,256]{1,0:T(4,128)S(1)}, f32[4,256]{1,0:T(4,128)S(1)}, f32[4,256,96]{1,2,0:T(8,128)S(1)}, bf16[2,256,384]{1,2,0:T(8,128)(2,1)}...) while((s32[]{:T(128)}, f32[4,256]{1,0:T(4,128)S(1)}, ...), condition=%wide.region_8.9_spmd, body=%wide.region_5.8_spmd.sunk | while | flops 103286784 | bytes 8003757 | solution.py:121
  153.4 4.9 collective-permute-start.1
  166.1 11.1 %collective-permute-start.1 = (s32[256]{0:T(256)}, s32[256]{0:T(256)S(1)}, u32[]{:S(2)}, u32[]{:S(2)}) collective-permute-start(s32[256]{0:T(256)} %get-tuple-element.160), channel_id=1, source_target_pairs={{0,8},{8,16},{16,24},{24,32},{32,40},{40,48},{48,56},{56,64},{64,7... | collective-permute-start | bytes 3080 | tf_op jit(solution)/shard_map/while/body/eval_jaxpr/ppermute | solution.py:26
  180.7 4.0 collective-permute-start
  184.7 11.4 %collective-permute-start.1 = (s32[256]{0:T(256)}, s32[256]{0:T(256)S(1)}, u32[]{:S(2)}, u32[]{:S(2)}) collective-permute-start(s32[256]{0:T(256)} %get-tuple-element.160), channel_id=1, source_target_pairs={{0,8},{8,16},{16,24},{24,32},{32,40},{40,48},{48,56},{56,64},{64,7... | collective-permute-start | bytes 3080 | tf_op jit(solution)/shard_map/while/body/eval_jaxpr/ppermute | solution.py:26
  199.6 4.0 collective-permute-start
  203.6 10.6 %collective-permute-start.1 = (s32[256]{0:T(256)}, s32[256]{0:T(256)S(1)}, u32[]{:S(2)}, u32[]{:S(2)}) collective-permute-start(s32[256]{0:T(256)} %get-tuple-element.160), channel_id=1, source_target_pairs={{0,8},{8,16},{16,24},{24,32},{32,40},{40,48},{48,56},{56,64},{64,7... | collective-permute-start | bytes 3080 | tf_op jit(solution)/shard_map/while/body/eval_jaxpr/ppermute | solution.py:26
  217.7 4.0 collective-permute-start
  221.7 9.3 %collective-permute-start.1 = (s32[256]{0:T(256)}, s32[256]{0:T(256)S(1)}, u32[]{:S(2)}, u32[]{:S(2)}) collective-permute-start(s32[256]{0:T(256)} %get-tuple-element.160), channel_id=1, source_target_pairs={{0,8},{8,16},{16,24},{24,32},{32,40},{40,48},{48,56},{56,64},{64,7... | collective-permute-start | bytes 3080 | tf_op jit(solution)/shard_map/while/body/eval_jaxpr/ppermute | solution.py:26
  234.4 4.0 collective-permute-start
  238.4 7.3 collective-permute-start.1
  249.3 4.0 collective-permute-start
  253.3 7.3 collective-permute-start.1
  264.1 4.0 collective-permute-start
  268.1 7.3 collective-permute-start.1
  278.9 4.0 collective-permute-start
  282.9 7.3 collective-permute-start.1
  293.8 4.0 collective-permute-start
  297.8 8.0 collective-permute-start.1
  309.3 4.0 collective-permute-start
  313.3 8.0 collective-permute-start.1
  324.9 4.0 collective-permute-start
  328.9 8.0 collective-permute-start.1
  340.4 4.0 collective-permute-start
  344.4 8.0 collective-permute-start.1
  355.9 4.0 collective-permute-start
  359.9 8.0 collective-permute-start.1
  371.4 4.0 collective-permute-start
  375.4 8.0 collective-permute-start.1
  390.9 8.0 collective-permute-start.1
  402.5 4.0 collective-permute-start
  406.4 8.0 collective-permute-start.1
  418.0 4.0 collective-permute-start
  422.0 8.0 collective-permute-start.1
  433.5 4.0 collective-permute-start
  437.5 8.0 collective-permute-start.1
  449.0 4.0 collective-permute-start
  453.0 8.0 collective-permute-start.1
  464.5 4.0 collective-permute-start
  468.5 8.0 collective-permute-start.1
  480.0 4.0 collective-permute-start
  484.0 8.0 collective-permute-start.1
  495.5 4.0 collective-permute-start
  499.5 8.0 collective-permute-start.1
  514.7 325.7 %all-gather.3.cloned.1.call-done = bf16[2048,3072]{1,0:T(8,128)(2,1)} async-done(((bf16[256,3072]{1,0:T(8,128)(2,1)}), bf16[2048,3072]{1,0:T(8,128)(2,1)}) %all-gather.3.cloned.1.call-update) | async-done | bytes 12582928 | tf_op jit(solution)/shard_map/all_gather | solution.py:17
  840.3 8.8 %reduce_sum.50 = bf16[256,3072]{1,0:T(8,128)(2,1)} reduce(bf16[8,256,3072]{2,1,0:T(8,128)(2,1)} %bitcast.37, bf16[]{:T(256)} %constant.16.clone.1), dimensions={0}, to_apply=%region_9.10 | reduce | flops 5505024 | bytes 14155778 | tf_op jit(solution)/shard_map/reduce_sum | solution.py:17
  850.2 18.5 %psum.7 = f32[256]{0:T(256)S(1)} all-reduce(f32[256]{0:T(256)S(1)} %get-tuple-element.66), channel_id=1, replica_groups=mesh['seq'=64,'tp'=8] {'tp'}, use_global_device_ids=true, to_apply=%region_11.12 | all-reduce | flops 256 | bytes 2048 | tf_op jit(solution)/shard_map/psum | solution.py:138
  (468 shorter events, 209.9 us)
Async XLA Ops:
  7.2 833.1 %all-gather.3.cloned.1.call-start = ((), (), s32[]{:S(2)}) async-start(), calls=%async_computation | async-start | bytes 14155776 | tf_op jit(solution)/shard_map/all_gather | solution.py:17
  45.1 10.0 %collective-permute-start = (bf16[2,256,384]{1,2,0:T(8,128)(2,1)}, bf16[2,256,384]{1,2,0:T(8,128)(2,1)S(1)}, u32[]{:S(2)}, u32[]{:S(2)}) collective-permute-start(bf16[2,256,384]{1,2,0:T(8,128)(2,1)} %get-tuple-element.159), channel_id=1, source_target_pairs={{0,8},{8,16},{16,24},{24,32},{32,40},{40,48},{48,56},{56,64},{64,7... | collective-permute-start | bytes 1179656 | tf_op jit(solution)/shard_map/while/body/eval_jaxpr/ppermute | solution.py:26
  56.9 10.0 %collective-permute-start = (bf16[2,256,384]{1,2,0:T(8,128)(2,1)}, bf16[2,256,384]{1,2,0:T(8,128)(2,1)S(1)}, u32[]{:S(2)}, u32[]{:S(2)}) collective-permute-start(bf16[2,256,384]{1,2,0:T(8,128)(2,1)} %get-tuple-element.159), channel_id=1, source_target_pairs={{0,8},{8,16},{16,24},{24,32},{32,40},{40,48},{48,56},{56,64},{64,7... | collective-permute-start | bytes 1179656 | tf_op jit(solution)/shard_map/while/body/eval_jaxpr/ppermute | solution.py:26
  68.7 10.0 %collective-permute-start = (bf16[2,256,384]{1,2,0:T(8,128)(2,1)}, bf16[2,256,384]{1,2,0:T(8,128)(2,1)S(1)}, u32[]{:S(2)}, u32[]{:S(2)}) collective-permute-start(bf16[2,256,384]{1,2,0:T(8,128)(2,1)} %get-tuple-element.159), channel_id=1, source_target_pairs={{0,8},{8,16},{16,24},{24,32},{32,40},{40,48},{48,56},{56,64},{64,7... | collective-permute-start | bytes 1179656 | tf_op jit(solution)/shard_map/while/body/eval_jaxpr/ppermute | solution.py:26
  80.5 10.0 %collective-permute-start = (bf16[2,256,384]{1,2,0:T(8,128)(2,1)}, bf16[2,256,384]{1,2,0:T(8,128)(2,1)S(1)}, u32[]{:S(2)}, u32[]{:S(2)}) collective-permute-start(bf16[2,256,384]{1,2,0:T(8,128)(2,1)} %get-tuple-element.159), channel_id=1, source_target_pairs={{0,8},{8,16},{16,24},{24,32},{32,40},{40,48},{48,56},{56,64},{64,7... | collective-permute-start | bytes 1179656 | tf_op jit(solution)/shard_map/while/body/eval_jaxpr/ppermute | solution.py:26
  92.4 10.0 %collective-permute-start = (bf16[2,256,384]{1,2,0:T(8,128)(2,1)}, bf16[2,256,384]{1,2,0:T(8,128)(2,1)S(1)}, u32[]{:S(2)}, u32[]{:S(2)}) collective-permute-start(bf16[2,256,384]{1,2,0:T(8,128)(2,1)} %get-tuple-element.159), channel_id=1, source_target_pairs={{0,8},{8,16},{16,24},{24,32},{32,40},{40,48},{48,56},{56,64},{64,7... | collective-permute-start | bytes 1179656 | tf_op jit(solution)/shard_map/while/body/eval_jaxpr/ppermute | solution.py:26
  104.2 10.0 %collective-permute-start = (bf16[2,256,384]{1,2,0:T(8,128)(2,1)}, bf16[2,256,384]{1,2,0:T(8,128)(2,1)S(1)}, u32[]{:S(2)}, u32[]{:S(2)}) collective-permute-start(bf16[2,256,384]{1,2,0:T(8,128)(2,1)} %get-tuple-element.159), channel_id=1, source_target_pairs={{0,8},{8,16},{16,24},{24,32},{32,40},{40,48},{48,56},{56,64},{64,7... | collective-permute-start | bytes 1179656 | tf_op jit(solution)/shard_map/while/body/eval_jaxpr/ppermute | solution.py:26
  116.0 10.0 %collective-permute-start = (bf16[2,256,384]{1,2,0:T(8,128)(2,1)}, bf16[2,256,384]{1,2,0:T(8,128)(2,1)S(1)}, u32[]{:S(2)}, u32[]{:S(2)}) collective-permute-start(bf16[2,256,384]{1,2,0:T(8,128)(2,1)} %get-tuple-element.159), channel_id=1, source_target_pairs={{0,8},{8,16},{16,24},{24,32},{32,40},{40,48},{48,56},{56,64},{64,7... | collective-permute-start | bytes 1179656 | tf_op jit(solution)/shard_map/while/body/eval_jaxpr/ppermute | solution.py:26
  127.8 10.0 %collective-permute-start = (bf16[2,256,384]{1,2,0:T(8,128)(2,1)}, bf16[2,256,384]{1,2,0:T(8,128)(2,1)S(1)}, u32[]{:S(2)}, u32[]{:S(2)}) collective-permute-start(bf16[2,256,384]{1,2,0:T(8,128)(2,1)} %get-tuple-element.159), channel_id=1, source_target_pairs={{0,8},{8,16},{16,24},{24,32},{32,40},{40,48},{48,56},{56,64},{64,7... | collective-permute-start | bytes 1179656 | tf_op jit(solution)/shard_map/while/body/eval_jaxpr/ppermute | solution.py:26
  139.6 10.0 %collective-permute-start = (bf16[2,256,384]{1,2,0:T(8,128)(2,1)}, bf16[2,256,384]{1,2,0:T(8,128)(2,1)S(1)}, u32[]{:S(2)}, u32[]{:S(2)}) collective-permute-start(bf16[2,256,384]{1,2,0:T(8,128)(2,1)} %get-tuple-element.159), channel_id=1, source_target_pairs={{0,8},{8,16},{16,24},{24,32},{32,40},{40,48},{48,56},{56,64},{64,7... | collective-permute-start | bytes 1179656 | tf_op jit(solution)/shard_map/while/body/eval_jaxpr/ppermute | solution.py:26
  151.5 10.0 %collective-permute-start = (bf16[2,256,384]{1,2,0:T(8,128)(2,1)}, bf16[2,256,384]{1,2,0:T(8,128)(2,1)S(1)}, u32[]{:S(2)}, u32[]{:S(2)}) collective-permute-start(bf16[2,256,384]{1,2,0:T(8,128)(2,1)} %get-tuple-element.159), channel_id=1, source_target_pairs={{0,8},{8,16},{16,24},{24,32},{32,40},{40,48},{48,56},{56,64},{64,7... | collective-permute-start | bytes 1179656 | tf_op jit(solution)/shard_map/while/body/eval_jaxpr/ppermute | solution.py:26
  163.3 15.6 %collective-permute-start = (bf16[2,256,384]{1,2,0:T(8,128)(2,1)}, bf16[2,256,384]{1,2,0:T(8,128)(2,1)S(1)}, u32[]{:S(2)}, u32[]{:S(2)}) collective-permute-start(bf16[2,256,384]{1,2,0:T(8,128)(2,1)} %get-tuple-element.159), channel_id=1, source_target_pairs={{0,8},{8,16},{16,24},{24,32},{32,40},{40,48},{48,56},{56,64},{64,7... | collective-permute-start | bytes 1179656 | tf_op jit(solution)/shard_map/while/body/eval_jaxpr/ppermute | solution.py:26
  166.1 12.1 %collective-permute-start.1 = (s32[256]{0:T(256)}, s32[256]{0:T(256)S(1)}, u32[]{:S(2)}, u32[]{:S(2)}) collective-permute-start(s32[256]{0:T(256)} %get-tuple-element.160), channel_id=1, source_target_pairs={{0,8},{8,16},{16,24},{24,32},{32,40},{40,48},{48,56},{56,64},{64,7... | collective-permute-start | bytes 3080 | tf_op jit(solution)/shard_map/while/body/eval_jaxpr/ppermute | solution.py:26
  180.7 17.1 %collective-permute-start = (bf16[2,256,384]{1,2,0:T(8,128)(2,1)}, bf16[2,256,384]{1,2,0:T(8,128)(2,1)S(1)}, u32[]{:S(2)}, u32[]{:S(2)}) collective-permute-start(bf16[2,256,384]{1,2,0:T(8,128)(2,1)} %get-tuple-element.159), channel_id=1, source_target_pairs={{0,8},{8,16},{16,24},{24,32},{32,40},{40,48},{48,56},{56,64},{64,7... | collective-permute-start | bytes 1179656 | tf_op jit(solution)/shard_map/while/body/eval_jaxpr/ppermute | solution.py:26
  184.7 12.4 %collective-permute-start.1 = (s32[256]{0:T(256)}, s32[256]{0:T(256)S(1)}, u32[]{:S(2)}, u32[]{:S(2)}) collective-permute-start(s32[256]{0:T(256)} %get-tuple-element.160), channel_id=1, source_target_pairs={{0,8},{8,16},{16,24},{24,32},{32,40},{40,48},{48,56},{56,64},{64,7... | collective-permute-start | bytes 3080 | tf_op jit(solution)/shard_map/while/body/eval_jaxpr/ppermute | solution.py:26
  199.6 16.3 %collective-permute-start = (bf16[2,256,384]{1,2,0:T(8,128)(2,1)}, bf16[2,256,384]{1,2,0:T(8,128)(2,1)S(1)}, u32[]{:S(2)}, u32[]{:S(2)}) collective-permute-start(bf16[2,256,384]{1,2,0:T(8,128)(2,1)} %get-tuple-element.159), channel_id=1, source_target_pairs={{0,8},{8,16},{16,24},{24,32},{32,40},{40,48},{48,56},{56,64},{64,7... | collective-permute-start | bytes 1179656 | tf_op jit(solution)/shard_map/while/body/eval_jaxpr/ppermute | solution.py:26
  203.6 11.6 %collective-permute-start.1 = (s32[256]{0:T(256)}, s32[256]{0:T(256)S(1)}, u32[]{:S(2)}, u32[]{:S(2)}) collective-permute-start(s32[256]{0:T(256)} %get-tuple-element.160), channel_id=1, source_target_pairs={{0,8},{8,16},{16,24},{24,32},{32,40},{40,48},{48,56},{56,64},{64,7... | collective-permute-start | bytes 3080 | tf_op jit(solution)/shard_map/while/body/eval_jaxpr/ppermute | solution.py:26
  217.7 14.9 %collective-permute-start = (bf16[2,256,384]{1,2,0:T(8,128)(2,1)}, bf16[2,256,384]{1,2,0:T(8,128)(2,1)S(1)}, u32[]{:S(2)}, u32[]{:S(2)}) collective-permute-start(bf16[2,256,384]{1,2,0:T(8,128)(2,1)} %get-tuple-element.159), channel_id=1, source_target_pairs={{0,8},{8,16},{16,24},{24,32},{32,40},{40,48},{48,56},{56,64},{64,7... | collective-permute-start | bytes 1179656 | tf_op jit(solution)/shard_map/while/body/eval_jaxpr/ppermute | solution.py:26
  221.7 10.3 %collective-permute-start.1 = (s32[256]{0:T(256)}, s32[256]{0:T(256)S(1)}, u32[]{:S(2)}, u32[]{:S(2)}) collective-permute-start(s32[256]{0:T(256)} %get-tuple-element.160), channel_id=1, source_target_pairs={{0,8},{8,16},{16,24},{24,32},{32,40},{40,48},{48,56},{56,64},{64,7... | collective-permute-start | bytes 3080 | tf_op jit(solution)/shard_map/while/body/eval_jaxpr/ppermute | solution.py:26
  234.4 13.0 %collective-permute-start = (bf16[2,256,384]{1,2,0:T(8,128)(2,1)}, bf16[2,256,384]{1,2,0:T(8,128)(2,1)S(1)}, u32[]{:S(2)}, u32[]{:S(2)}) collective-permute-start(bf16[2,256,384]{1,2,0:T(8,128)(2,1)} %get-tuple-element.159), channel_id=1, source_target_pairs={{0,8},{8,16},{16,24},{24,32},{32,40},{40,48},{48,56},{56,64},{64,7... | collective-permute-start | bytes 1179656 | tf_op jit(solution)/shard_map/while/body/eval_jaxpr/ppermute | solution.py:26
  249.3 13.0 %collective-permute-start = (bf16[2,256,384]{1,2,0:T(8,128)(2,1)}, bf16[2,256,384]{1,2,0:T(8,128)(2,1)S(1)}, u32[]{:S(2)}, u32[]{:S(2)}) collective-permute-start(bf16[2,256,384]{1,2,0:T(8,128)(2,1)} %get-tuple-element.159), channel_id=1, source_target_pairs={{0,8},{8,16},{16,24},{24,32},{32,40},{40,48},{48,56},{56,64},{64,7... | collective-permute-start | bytes 1179656 | tf_op jit(solution)/shard_map/while/body/eval_jaxpr/ppermute | solution.py:26
  264.1 13.0 %collective-permute-start = (bf16[2,256,384]{1,2,0:T(8,128)(2,1)}, bf16[2,256,384]{1,2,0:T(8,128)(2,1)S(1)}, u32[]{:S(2)}, u32[]{:S(2)}) collective-permute-start(bf16[2,256,384]{1,2,0:T(8,128)(2,1)} %get-tuple-element.159), channel_id=1, source_target_pairs={{0,8},{8,16},{16,24},{24,32},{32,40},{40,48},{48,56},{56,64},{64,7... | collective-permute-start | bytes 1179656 | tf_op jit(solution)/shard_map/while/body/eval_jaxpr/ppermute | solution.py:26
  278.9 13.0 %collective-permute-start = (bf16[2,256,384]{1,2,0:T(8,128)(2,1)}, bf16[2,256,384]{1,2,0:T(8,128)(2,1)S(1)}, u32[]{:S(2)}, u32[]{:S(2)}) collective-permute-start(bf16[2,256,384]{1,2,0:T(8,128)(2,1)} %get-tuple-element.159), channel_id=1, source_target_pairs={{0,8},{8,16},{16,24},{24,32},{32,40},{40,48},{48,56},{56,64},{64,7... | collective-permute-start | bytes 1179656 | tf_op jit(solution)/shard_map/while/body/eval_jaxpr/ppermute | solution.py:26
  293.8 13.7 %collective-permute-start = (bf16[2,256,384]{1,2,0:T(8,128)(2,1)}, bf16[2,256,384]{1,2,0:T(8,128)(2,1)S(1)}, u32[]{:S(2)}, u32[]{:S(2)}) collective-permute-start(bf16[2,256,384]{1,2,0:T(8,128)(2,1)} %get-tuple-element.159), channel_id=1, source_target_pairs={{0,8},{8,16},{16,24},{24,32},{32,40},{40,48},{48,56},{56,64},{64,7... | collective-permute-start | bytes 1179656 | tf_op jit(solution)/shard_map/while/body/eval_jaxpr/ppermute | solution.py:26
  297.8 9.1 %collective-permute-start.1 = (s32[256]{0:T(256)}, s32[256]{0:T(256)S(1)}, u32[]{:S(2)}, u32[]{:S(2)}) collective-permute-start(s32[256]{0:T(256)} %get-tuple-element.160), channel_id=1, source_target_pairs={{0,8},{8,16},{16,24},{24,32},{32,40},{40,48},{48,56},{56,64},{64,7... | collective-permute-start | bytes 3080 | tf_op jit(solution)/shard_map/while/body/eval_jaxpr/ppermute | solution.py:26
  309.3 13.7 %collective-permute-start = (bf16[2,256,384]{1,2,0:T(8,128)(2,1)}, bf16[2,256,384]{1,2,0:T(8,128)(2,1)S(1)}, u32[]{:S(2)}, u32[]{:S(2)}) collective-permute-start(bf16[2,256,384]{1,2,0:T(8,128)(2,1)} %get-tuple-element.159), channel_id=1, source_target_pairs={{0,8},{8,16},{16,24},{24,32},{32,40},{40,48},{48,56},{56,64},{64,7... | collective-permute-start | bytes 1179656 | tf_op jit(solution)/shard_map/while/body/eval_jaxpr/ppermute | solution.py:26
  313.3 9.0 %collective-permute-start.1 = (s32[256]{0:T(256)}, s32[256]{0:T(256)S(1)}, u32[]{:S(2)}, u32[]{:S(2)}) collective-permute-start(s32[256]{0:T(256)} %get-tuple-element.160), channel_id=1, source_target_pairs={{0,8},{8,16},{16,24},{24,32},{32,40},{40,48},{48,56},{56,64},{64,7... | collective-permute-start | bytes 3080 | tf_op jit(solution)/shard_map/while/body/eval_jaxpr/ppermute | solution.py:26
  324.9 13.7 %collective-permute-start = (bf16[2,256,384]{1,2,0:T(8,128)(2,1)}, bf16[2,256,384]{1,2,0:T(8,128)(2,1)S(1)}, u32[]{:S(2)}, u32[]{:S(2)}) collective-permute-start(bf16[2,256,384]{1,2,0:T(8,128)(2,1)} %get-tuple-element.159), channel_id=1, source_target_pairs={{0,8},{8,16},{16,24},{24,32},{32,40},{40,48},{48,56},{56,64},{64,7... | collective-permute-start | bytes 1179656 | tf_op jit(solution)/shard_map/while/body/eval_jaxpr/ppermute | solution.py:26
  328.9 9.0 %collective-permute-start.1 = (s32[256]{0:T(256)}, s32[256]{0:T(256)S(1)}, u32[]{:S(2)}, u32[]{:S(2)}) collective-permute-start(s32[256]{0:T(256)} %get-tuple-element.160), channel_id=1, source_target_pairs={{0,8},{8,16},{16,24},{24,32},{32,40},{40,48},{48,56},{56,64},{64,7... | collective-permute-start | bytes 3080 | tf_op jit(solution)/shard_map/while/body/eval_jaxpr/ppermute | solution.py:26
  340.4 13.7 %collective-permute-start = (bf16[2,256,384]{1,2,0:T(8,128)(2,1)}, bf16[2,256,384]{1,2,0:T(8,128)(2,1)S(1)}, u32[]{:S(2)}, u32[]{:S(2)}) collective-permute-start(bf16[2,256,384]{1,2,0:T(8,128)(2,1)} %get-tuple-element.159), channel_id=1, source_target_pairs={{0,8},{8,16},{16,24},{24,32},{32,40},{40,48},{48,56},{56,64},{64,7... | collective-permute-start | bytes 1179656 | tf_op jit(solution)/shard_map/while/body/eval_jaxpr/ppermute | solution.py:26
  344.4 9.0 %collective-permute-start.1 = (s32[256]{0:T(256)}, s32[256]{0:T(256)S(1)}, u32[]{:S(2)}, u32[]{:S(2)}) collective-permute-start(s32[256]{0:T(256)} %get-tuple-element.160), channel_id=1, source_target_pairs={{0,8},{8,16},{16,24},{24,32},{32,40},{40,48},{48,56},{56,64},{64,7... | collective-permute-start | bytes 3080 | tf_op jit(solution)/shard_map/while/body/eval_jaxpr/ppermute | solution.py:26
  355.9 13.7 %collective-permute-start = (bf16[2,256,384]{1,2,0:T(8,128)(2,1)}, bf16[2,256,384]{1,2,0:T(8,128)(2,1)S(1)}, u32[]{:S(2)}, u32[]{:S(2)}) collective-permute-start(bf16[2,256,384]{1,2,0:T(8,128)(2,1)} %get-tuple-element.159), channel_id=1, source_target_pairs={{0,8},{8,16},{16,24},{24,32},{32,40},{40,48},{48,56},{56,64},{64,7... | collective-permute-start | bytes 1179656 | tf_op jit(solution)/shard_map/while/body/eval_jaxpr/ppermute | solution.py:26
  359.9 9.0 %collective-permute-start.1 = (s32[256]{0:T(256)}, s32[256]{0:T(256)S(1)}, u32[]{:S(2)}, u32[]{:S(2)}) collective-permute-start(s32[256]{0:T(256)} %get-tuple-element.160), channel_id=1, source_target_pairs={{0,8},{8,16},{16,24},{24,32},{32,40},{40,48},{48,56},{56,64},{64,7... | collective-permute-start | bytes 3080 | tf_op jit(solution)/shard_map/while/body/eval_jaxpr/ppermute | solution.py:26
  371.4 13.7 %collective-permute-start = (bf16[2,256,384]{1,2,0:T(8,128)(2,1)}, bf16[2,256,384]{1,2,0:T(8,128)(2,1)S(1)}, u32[]{:S(2)}, u32[]{:S(2)}) collective-permute-start(bf16[2,256,384]{1,2,0:T(8,128)(2,1)} %get-tuple-element.159), channel_id=1, source_target_pairs={{0,8},{8,16},{16,24},{24,32},{32,40},{40,48},{48,56},{56,64},{64,7... | collective-permute-start | bytes 1179656 | tf_op jit(solution)/shard_map/while/body/eval_jaxpr/ppermute | solution.py:26
  375.4 9.0 %collective-permute-start.1 = (s32[256]{0:T(256)}, s32[256]{0:T(256)S(1)}, u32[]{:S(2)}, u32[]{:S(2)}) collective-permute-start(s32[256]{0:T(256)} %get-tuple-element.160), channel_id=1, source_target_pairs={{0,8},{8,16},{16,24},{24,32},{32,40},{40,48},{48,56},{56,64},{64,7... | collective-permute-start | bytes 3080 | tf_op jit(solution)/shard_map/while/body/eval_jaxpr/ppermute | solution.py:26
  386.9 13.7 %collective-permute-start = (bf16[2,256,384]{1,2,0:T(8,128)(2,1)}, bf16[2,256,384]{1,2,0:T(8,128)(2,1)S(1)}, u32[]{:S(2)}, u32[]{:S(2)}) collective-permute-start(bf16[2,256,384]{1,2,0:T(8,128)(2,1)} %get-tuple-element.159), channel_id=1, source_target_pairs={{0,8},{8,16},{16,24},{24,32},{32,40},{40,48},{48,56},{56,64},{64,7... | collective-permute-start | bytes 1179656 | tf_op jit(solution)/shard_map/while/body/eval_jaxpr/ppermute | solution.py:26
  390.9 9.0 %collective-permute-start.1 = (s32[256]{0:T(256)}, s32[256]{0:T(256)S(1)}, u32[]{:S(2)}, u32[]{:S(2)}) collective-permute-start(s32[256]{0:T(256)} %get-tuple-element.160), channel_id=1, source_target_pairs={{0,8},{8,16},{16,24},{24,32},{32,40},{40,48},{48,56},{56,64},{64,7... | collective-permute-start | bytes 3080 | tf_op jit(solution)/shard_map/while/body/eval_jaxpr/ppermute | solution.py:26
  402.5 13.7 %collective-permute-start = (bf16[2,256,384]{1,2,0:T(8,128)(2,1)}, bf16[2,256,384]{1,2,0:T(8,128)(2,1)S(1)}, u32[]{:S(2)}, u32[]{:S(2)}) collective-permute-start(bf16[2,256,384]{1,2,0:T(8,128)(2,1)} %get-tuple-element.159), channel_id=1, source_target_pairs={{0,8},{8,16},{16,24},{24,32},{32,40},{40,48},{48,56},{56,64},{64,7... | collective-permute-start | bytes 1179656 | tf_op jit(solution)/shard_map/while/body/eval_jaxpr/ppermute | solution.py:26
  406.4 9.0 %collective-permute-start.1 = (s32[256]{0:T(256)}, s32[256]{0:T(256)S(1)}, u32[]{:S(2)}, u32[]{:S(2)}) collective-permute-start(s32[256]{0:T(256)} %get-tuple-element.160), channel_id=1, source_target_pairs={{0,8},{8,16},{16,24},{24,32},{32,40},{40,48},{48,56},{56,64},{64,7... | collective-permute-start | bytes 3080 | tf_op jit(solution)/shard_map/while/body/eval_jaxpr/ppermute | solution.py:26
  418.0 13.7 %collective-permute-start = (bf16[2,256,384]{1,2,0:T(8,128)(2,1)}, bf16[2,256,384]{1,2,0:T(8,128)(2,1)S(1)}, u32[]{:S(2)}, u32[]{:S(2)}) collective-permute-start(bf16[2,256,384]{1,2,0:T(8,128)(2,1)} %get-tuple-element.159), channel_id=1, source_target_pairs={{0,8},{8,16},{16,24},{24,32},{32,40},{40,48},{48,56},{56,64},{64,7... | collective-permute-start | bytes 1179656 | tf_op jit(solution)/shard_map/while/body/eval_jaxpr/ppermute | solution.py:26
  433.5 13.7 %collective-permute-start = (bf16[2,256,384]{1,2,0:T(8,128)(2,1)}, bf16[2,256,384]{1,2,0:T(8,128)(2,1)S(1)}, u32[]{:S(2)}, u32[]{:S(2)}) collective-permute-start(bf16[2,256,384]{1,2,0:T(8,128)(2,1)} %get-tuple-element.159), channel_id=1, source_target_pairs={{0,8},{8,16},{16,24},{24,32},{32,40},{40,48},{48,56},{56,64},{64,7... | collective-permute-start | bytes 1179656 | tf_op jit(solution)/shard_map/while/body/eval_jaxpr/ppermute | solution.py:26
  449.0 13.7 %collective-permute-start = (bf16[2,256,384]{1,2,0:T(8,128)(2,1)}, bf16[2,256,384]{1,2,0:T(8,128)(2,1)S(1)}, u32[]{:S(2)}, u32[]{:S(2)}) collective-permute-start(bf16[2,256,384]{1,2,0:T(8,128)(2,1)} %get-tuple-element.159), channel_id=1, source_target_pairs={{0,8},{8,16},{16,24},{24,32},{32,40},{40,48},{48,56},{56,64},{64,7... | collective-permute-start | bytes 1179656 | tf_op jit(solution)/shard_map/while/body/eval_jaxpr/ppermute | solution.py:26
  464.5 13.7 %collective-permute-start = (bf16[2,256,384]{1,2,0:T(8,128)(2,1)}, bf16[2,256,384]{1,2,0:T(8,128)(2,1)S(1)}, u32[]{:S(2)}, u32[]{:S(2)}) collective-permute-start(bf16[2,256,384]{1,2,0:T(8,128)(2,1)} %get-tuple-element.159), channel_id=1, source_target_pairs={{0,8},{8,16},{16,24},{24,32},{32,40},{40,48},{48,56},{56,64},{64,7... | collective-permute-start | bytes 1179656 | tf_op jit(solution)/shard_map/while/body/eval_jaxpr/ppermute | solution.py:26
  468.5 9.0 %collective-permute-start.1 = (s32[256]{0:T(256)}, s32[256]{0:T(256)S(1)}, u32[]{:S(2)}, u32[]{:S(2)}) collective-permute-start(s32[256]{0:T(256)} %get-tuple-element.160), channel_id=1, source_target_pairs={{0,8},{8,16},{16,24},{24,32},{32,40},{40,48},{48,56},{56,64},{64,7... | collective-permute-start | bytes 3080 | tf_op jit(solution)/shard_map/while/body/eval_jaxpr/ppermute | solution.py:26
  480.0 13.7 %collective-permute-start = (bf16[2,256,384]{1,2,0:T(8,128)(2,1)}, bf16[2,256,384]{1,2,0:T(8,128)(2,1)S(1)}, u32[]{:S(2)}, u32[]{:S(2)}) collective-permute-start(bf16[2,256,384]{1,2,0:T(8,128)(2,1)} %get-tuple-element.159), channel_id=1, source_target_pairs={{0,8},{8,16},{16,24},{24,32},{32,40},{40,48},{48,56},{56,64},{64,7... | collective-permute-start | bytes 1179656 | tf_op jit(solution)/shard_map/while/body/eval_jaxpr/ppermute | solution.py:26
  484.0 9.0 %collective-permute-start.1 = (s32[256]{0:T(256)}, s32[256]{0:T(256)S(1)}, u32[]{:S(2)}, u32[]{:S(2)}) collective-permute-start(s32[256]{0:T(256)} %get-tuple-element.160), channel_id=1, source_target_pairs={{0,8},{8,16},{16,24},{24,32},{32,40},{40,48},{48,56},{56,64},{64,7... | collective-permute-start | bytes 3080 | tf_op jit(solution)/shard_map/while/body/eval_jaxpr/ppermute | solution.py:26
  495.5 13.7 %collective-permute-start = (bf16[2,256,384]{1,2,0:T(8,128)(2,1)}, bf16[2,256,384]{1,2,0:T(8,128)(2,1)S(1)}, u32[]{:S(2)}, u32[]{:S(2)}) collective-permute-start(bf16[2,256,384]{1,2,0:T(8,128)(2,1)} %get-tuple-element.159), channel_id=1, source_target_pairs={{0,8},{8,16},{16,24},{24,32},{32,40},{40,48},{48,56},{56,64},{64,7... | collective-permute-start | bytes 1179656 | tf_op jit(solution)/shard_map/while/body/eval_jaxpr/ppermute | solution.py:26
  499.5 9.0 %collective-permute-start.1 = (s32[256]{0:T(256)}, s32[256]{0:T(256)S(1)}, u32[]{:S(2)}, u32[]{:S(2)}) collective-permute-start(s32[256]{0:T(256)} %get-tuple-element.160), channel_id=1, source_target_pairs={{0,8},{8,16},{16,24},{24,32},{32,40},{40,48},{48,56},{56,64},{64,7... | collective-permute-start | bytes 3080 | tf_op jit(solution)/shard_map/while/body/eval_jaxpr/ppermute | solution.py:26
  (30 other events, 1078.9 us)
Sparse Core Ops, SparseCore 0:
  513.4 326.8 all-gather.2
